TPU v7x, 256 devices: a whole 4x4x8 slice. The times are simulated.
256 devices in a mesh: seq: 64 (over x, z, core), tensor: 4 (over y).
Axes of the slice: x: 4, y: 4, z: 8, core: 2. Of those that a mesh axis runs over, the one named last changes fastest.
Arguments:
- hidden: bfloat16 [512, 1280], P('seq', 'tensor'), may hold values from -20 to 20
- inward_weight: bfloat16 [1280, 3, 1280], P(None, None, 'tensor'), may hold values from -0.15625 to 0.15625
- output_weight: bfloat16 [1280, 1280], P('tensor'), may hold values from -0.559017 to 0.559017
- score_gain: float32 [1280], P('tensor'), may hold values from 0.5 to 9
- eigen_rate: float32 [1280], replicated, may hold values from 0.1 to 0.6
- lengths: int32 [512], replicated, may hold values from 1 to 16384, as said below
- page_request: int32 [1536], P('seq'), may hold values from 0 to 511, as said below
- page_number: int32 [1536], P('seq'), may hold values from 0 to 128, as said below
- page_cache: bfloat16 [1536, 128, 2, 1280], P('seq', None, None, 'tensor'), may hold values from -6 to 6
Outputs:
- new_hidden: bfloat16 [512, 1280], P('seq', 'tensor')
Inputs may be any that keep to these rules, and one draw needn't show every extreme that they name: `lengths`: exactly 4 requests have more than 256 cached positions; they have more than 16256, one has exactly 16384. Every other request has at most 256, one exactly 256. `page_request`: each page of each request stands in exactly one slot: pages 0 to 1 of every short request, pages 0 to 127 of every long request. The remaining 2 * 4 slots name a long request with page number 128 and hold nothing live. `page_number`: see page_request.
All inputs are finite; a program needn't handle non-finite values.
Results may differ from a plain program's by a relative error of at most 0.012.
The roundings to bfloat16 on the way count: a program that leaves them out, or rounds other values in their place, can miss the bound.
Values may be sent and summed in bfloat16 or wider, within the bound.
No kernel may reach another device: no remote copies, remote signals or barrier semaphores. Data moves between devices by JAX's collectives and lax.ppermute only.
A program may use at most 192 MiB of HBM per device.

v0:
```python
import math
import jax
import jax.numpy as jnp
from jax import lax
from jax.sharding import PartitionSpec as P

HEAD_DIM = 64
epsilon = 1e-06
far_below = -1e30


def head_norm(values, gain):
    shaped = values.reshape(values.shape[:-1] + (-1, HEAD_DIM))
    normed = shaped / jnp.sqrt(jnp.mean(shaped * shaped, axis=-1, keepdims=True) + epsilon)
    return normed * gain.reshape(-1, HEAD_DIM)


def scale_heads(summed, factor):
    shaped = summed.reshape(summed.shape[:-1] + (factor.shape[-1], -1))
    return (shaped * factor[..., None]).reshape(summed.shape)


def local(
    hidden,
    inward_weight,
    output_weight,
    score_gain,
    eigen_rate,
    lengths,
    page_request,
    page_number,
    page_cache,
):
    rows, width_local = hidden.shape
    heads_local = width_local // HEAD_DIM
    gathered = lax.all_gather(hidden, "tensor", axis=1, tiled=True)
    projected = jnp.dot(
        gathered,
        inward_weight.reshape(inward_weight.shape[0], -1),
        preferred_element_type=jnp.float32,
    )
    query = head_norm(projected[:, :width_local], score_gain).astype(jnp.bfloat16)
    key_new = head_norm(projected[:, width_local : 2 * width_local], score_gain).astype(
        jnp.bfloat16
    )
    value_own = projected[:, 2 * width_local :].astype(jnp.bfloat16)
    own_score = jnp.sum(
        (query.astype(jnp.float32) * key_new.astype(jnp.float32)).reshape(
            rows, heads_local, HEAD_DIM
        ),
        axis=-1,
    ) / math.sqrt(HEAD_DIM)
    all_queries = lax.all_gather(query, "seq", axis=0, tiled=True)
    pages, page_len = (page_cache.shape[0], page_cache.shape[1])
    owner_query = all_queries[page_request].reshape(pages, heads_local, HEAD_DIM)
    keys_scaled = head_norm(page_cache[:, :, 0, :].astype(jnp.float32), score_gain).astype(
        jnp.bfloat16
    )
    values_paged = page_cache[:, :, 1, :].reshape(pages, page_len, heads_local, HEAD_DIM)
    scores = jnp.einsum(
        "sphd,shd->shp", keys_scaled, owner_query, preferred_element_type=jnp.float32
    ) / math.sqrt(HEAD_DIM)
    positions = page_number[:, None] * page_len + jnp.arange(page_len, dtype=jnp.int32)[None, :]
    live_mask = positions < lengths[page_request][:, None]
    page_max = jnp.max(jnp.where(live_mask[:, None, :], scores, far_below), axis=-1)
    weights = jnp.where(live_mask[:, None, :], jnp.exp(scores - page_max[..., None]), 0.0).astype(
        jnp.bfloat16
    )
    page_total = jnp.sum(weights.astype(jnp.float32), axis=-1)
    page_acc = jnp.einsum(
        "shp,sphd->shd", weights, values_paged, preferred_element_type=jnp.float32
    ).reshape(pages, width_local)
    packed = jnp.concatenate(
        [page_acc, page_total, page_max, page_request.astype(jnp.float32)[:, None]], axis=1
    )
    all_parts = lax.all_gather(packed, "seq", axis=0, tiled=True)
    acc_all = all_parts[:, :width_local]
    total_all = all_parts[:, width_local : width_local + heads_local]
    max_all = all_parts[:, width_local + heads_local : width_local + 2 * heads_local]
    owner_all = all_parts[:, width_local + 2 * heads_local]
    first_row = lax.axis_index("seq") * rows
    row_ids = (first_row + jnp.arange(rows, dtype=jnp.int32)).astype(jnp.float32)
    mine = owner_all[None, :] == row_ids[:, None]
    masked_max = jnp.max(jnp.where(mine[:, :, None], max_all[None], far_below), axis=1)
    final_max = jnp.maximum(masked_max, own_score)
    factor = jnp.where(mine[:, :, None], jnp.exp(max_all[None] - final_max[:, None, :]), 0.0)
    own_factor = jnp.exp(own_score - final_max)
    total = jnp.sum(factor * total_all[None], axis=1) + own_factor
    stored = jnp.einsum(
        "rsh,shd->rhd",
        factor,
        acc_all.reshape(-1, heads_local, HEAD_DIM),
        precision=lax.Precision.HIGHEST,
    ).reshape(rows, width_local)
    summed = stored + scale_heads(value_own.astype(jnp.float32), own_factor)
    attended = (
        (summed.reshape(rows, heads_local, HEAD_DIM) / total[..., None])
        .reshape(rows, width_local)
        .astype(jnp.bfloat16)
    )
    partial_out = jnp.dot(attended, output_weight, preferred_element_type=jnp.float32)
    attn_out = lax.psum(partial_out, "tensor")
    width = attn_out.shape[1]
    state = gathered.astype(jnp.float32)
    unit = attn_out / jnp.sqrt(
        jnp.sum(attn_out * attn_out, axis=-1, keepdims=True) / width + epsilon
    )
    mixed = state + eigen_rate * (unit - state)
    result = mixed / jnp.sqrt(jnp.sum(mixed * mixed, axis=-1, keepdims=True) / width + epsilon)
    first_col = lax.axis_index("tensor") * width_local
    return lax.dynamic_slice_in_dim(result, first_col, width_local, 1).astype(jnp.bfloat16)


def solution(mesh):
    placed = (
        P("seq", "tensor"),
        P(None, None, "tensor"),
        P("tensor", None),
        P("tensor"),
        P(),
        P(),
        P("seq"),
        P("seq"),
        P("seq", None, None, "tensor"),
    )
    return jax.shard_map(
        local, mesh=mesh, in_specs=placed, out_specs=P("seq", "tensor"), check_vma=False
    )
```

profile of v0, /device:TPU:4, one launch (start us, length us, event | category | flops | bytes accessed | tf_op | source)
XLA Modules:
  0.0 202.5 jit_solution(14112942308790230901)
XLA Ops:
  6.5 0.8 broadcast_multiply_fusion
  7.3 0.7 compare_select_fusion
  8.1 0.8 mul.86
  8.8 12.7 %all-gather = bf16[4,320,8]{1,2,0:T(8,128)(2,1)S(1)} all-gather(bf16[1,320,8]{1,2,0:T(8,128)(2,1)} %bitcast.52), channel_id=1, replica_groups=mesh['seq'=64,'tensor'=4] {'tensor'}, dimensions={0}, use_global_device_ids=true | all-gather | bytes 25600 | tf_op jit(solution)/shard_map/all_gather | solution.py:36
  21.7 0.7 fusion.21
  22.5 0.6 copy-done.3
  23.6 53.2 %all_gather.10 = bf16[512,5,64]{2,0,1:T(8,128)(2,1)S(1)} all-gather(bf16[8,5,64]{2,0,1:T(8,128)(2,1)S(1)} %copy.50), channel_id=1, replica_groups=mesh['seq'=64,'tensor'=4] {'seq'}, dimensions={0}, use_global_device_ids=true | all-gather | bytes 332800 | tf_op jit(solution)/shard_map/all_gather | solution.py:53
  76.8 0.5 copy.51
  77.2 0.7 gather_fusion
  78.0 1.2 gather_fusion.1
  79.2 3.7 %fusion.18 = (bf16[24,128,1,320]{1,3,2,0:T(8,128)(2,1)}, bf16[24,128,1,320]{1,3,2,0:T(8,128)(2,1)S(1)}) fusion(bf16[24,128,2,320]{1,3,2,0:T(8,128)(2,1)} %param.17), kind=kLoop, calls=%fused_computation.58 | loop fusion | bytes 7864320 | tf_op jit(solution)/shard_map/slice | solution.py:59
  82.8 0.7 fusion
  83.7 0.7 fusion.3
  85.0 2.6 %fusion.9 = f32[24,5,1,64]{3,2,1,0:T(1,128)S(1)} fusion(bf16[24,128,5,64]{1,3,2,0:T(8,128)(2,1)} %bitcast.49, bf16[24,5,128,1]{2,0,1,3:T(8,128)(2,1)S(1)} %get-tuple-element.15), kind=kOutput, calls=%fused_computation.20 | convolution fusion | flops 1966080 | bytes 2027520 | tf_op jit(solution)/shard_map/shp,sphd->shd/dot_general | solution.py:70
  87.7 0.7 pad_maximum_fusion
  88.5 74.1 %all-gather.3.cloned.1.call-done = f32[1536,331]{1,0:T(8,128)} async-done(((f32[24,331]{1,0:T(8,128)}), f32[1536,331]{1,0:T(8,128)}) %all-gather.3.cloned.1.call-update) | async-done | bytes 2033680 | tf_op jit(solution)/shard_map/all_gather | solution.py:76
  162.7 3.0 %fusion.19 = (f32[1536,5]{1,0:T(8,128)}, f32[1536,5]{1,0:T(8,128)S(1)}) fusion(f32[1536,331]{1,0:T(8,128)} %all-gather.3.cloned.1.call-done), kind=kLoop, calls=%fused_computation.59 | loop fusion | bytes 122880 | tf_op jit(solution)/shard_map/slice | solution.py:79
  165.6 1.4 copy.56
  167.3 1.6 slice_reduce_fusion
  169.8 3.0 %copy.55 = f32[1536,320]{0,1:T(8,128)} copy(f32[1536,320]{1,0:T(8,128)} %bitcast.45) | data formatting | bytes 3932160 | tf_op jit(solution)/shard_map/slice | solution.py:77
  172.9 3.3 %convolution_bitcast_fusion = f32[8,5,64]{2,0,1:T(8,128)S(1)} fusion(f32[1536,5,64]{0,2,1:T(8,128)} %bitcast.46, f32[8,5]{0,1:T(8,128)S(1)} %multiply_maximum_fusion, f32[1536,5]{0,1:T(8,128)S(1)} %copy.56, pred[8,1536]{1,0:T(8,128)(4,1)S(1)} %broadcast_compare_fusion), kind=kOutput, calls=%fused_computation.8 | convolution fusion | flops 47308800 | bytes 2019488 | tf_op jit(solution)/shard_map/rsh,shd->rhd/dot_general | solution.py:89
  176.3 0.9 fusion.14
  177.2 17.4 %psum.7 = f32[8,1280]{1,0:T(8,128)S(1)} all-reduce(f32[8,1280]{1,0:T(8,128)S(1)} %fusion.14), channel_id=1, replica_groups=mesh['seq'=64,'tensor'=4] {'tensor'}, use_global_device_ids=true, to_apply=%region_8.9 | all-reduce | flops 10240 | bytes 81920 | tf_op jit(solution)/shard_map/psum | solution.py:102
  194.9 0.7 fusion.13
  (53 shorter events, 3.1 us)
Async XLA Ops:
  6.5 15.1 %copy-start = (bf16[1280,3,320]{0,2,1:T(8,128)(2,1)S(1)}, bf16[1280,3,320]{0,2,1:T(8,128)(2,1)}, u32[]{:S(2)}) copy-start(bf16[1280,3,320]{0,2,1:T(8,128)(2,1)} %param.10) | copy-start | bytes 7372804
  6.5 156.1 %all-gather.3.cloned.1.call-start = ((), (), s32[]{:S(2)}) async-start(), calls=%async_computation | async-start | bytes 2396160 | tf_op jit(solution)/shard_map/all_gather | solution.py:76
  21.6 55.6 %copy-start.1 = (s32[512]{0:T(512)S(1)}, s32[512]{0:T(512)}, u32[]{:S(2)}) copy-start(s32[512]{0:T(512)} %param.14) | copy-start | bytes 6148
  22.4 0.6 copy-start.3
  79.2 4.5 %copy-start.4 = (bf16[24,5,64]{2,1,0:T(8,128)(2,1)S(1)}, bf16[24,5,64]{2,1,0:T(8,128)(2,1)}, u32[]{:S(2)}) copy-start(bf16[24,5,64]{2,1,0:T(8,128)(2,1)} %gather_fusion.1) | copy-start | bytes 46084
  169.8 6.5 %copy-start.2 = (bf16[320,1280]{1,0:T(8,128)(2,1)S(1)}, bf16[320,1280]{1,0:T(8,128)(2,1)}, u32[]{:S(2)}) copy-start(bf16[320,1280]{1,0:T(8,128)(2,1)} %param.11) | copy-start | bytes 2457604
  172.9 21.8 %copy-start.5 = (f32[1280]{0:T(1024)S(1)}, f32[1280]{0:T(1024)}, u32[]{:S(2)}) copy-start(f32[1280]{0:T(1024)} %param.13) | copy-start | bytes 15364
Sparse Core Ops, SparseCore 0:
  88.6 74.0 all-gather.2
where the time goes:
time: 203 us; the launch traced here: 202 us
  blocking collectives  83.2 us (41%)
  waiting for transfers between devices  74.1 us (37%)
  local copies, waits for them, and re-layouts  18 us (9%)
  between operations  13.5 us (7%)
  matrix products  8.35 us (4%)
  other arithmetic  5.14 us (3%)
    all_gather x1, waiting for transfers between devices, local(): all_parts = lax.all_gather(packed, 'seq', axis=0, tiled=True)  74.1 us
    all_gather x1, blocking collectives, local(): all_queries = lax.all_gather(query, 'seq', axis=0, tiled=True)  53.2 us
    psum x1, blocking collectives, local(): attn_out = lax.psum(partial_out, 'tensor')  17.4 us
    all_gather x1, blocking collectives, local(): gathered = lax.all_gather(hidden, 'tensor', axis=1, tiled=True)  12.7 us
    slice x2, local copies, waits for them, and re-layouts, local(): all_parts[:, width_local + heads_local:width_local + 2 * heads_local]  4.38 us
  transfers between devices with their start and end apart: 1, of which 1 were waited for; matrix products, arithmetic and copies ran while one was open for 0% of the time, Pallas kernels for 0%

commit v1 on v0

--- a/solution.py
+++ b/solution.py
@@ -50,7 +50,9 @@
         ),
         axis=-1,
     ) / math.sqrt(HEAD_DIM)
-    all_queries = lax.all_gather(query, "seq", axis=0, tiled=True)
+    all_queries = jnp.concatenate(
+        lax.all_to_all(jnp.stack([query for _ in range(lax.axis_size("seq"))]), "seq", 0, 0), 0
+    )
     pages, page_len = (page_cache.shape[0], page_cache.shape[1])
     owner_query = all_queries[page_request].reshape(pages, heads_local, HEAD_DIM)
     keys_scaled = head_norm(page_cache[:, :, 0, :].astype(jnp.float32), score_gain).astype(

time: 203 us -> 170 us (0.84)
  blocking collectives: 83.2 us -> 30 us
  starting transfers between devices: 0.01 us -> 12.1 us
  waiting for transfers between devices: 74.1 us -> 77.9 us
  local copies, waits for them, and re-layouts: 18 us -> 20.5 us
    all_gather x1 -> x0, blocking collectives: 53.2 us -> none  [local(): all_queries = lax.all_gather(query, 'seq', axis=0, tiled=True)]
    all_to_all x0 -> x1, starting transfers between devices: none -> 12.1 us  [local(): lax.all_to_all(jnp.stack([query for _ in range(lax.axis_size('seq'))]), '...]
    all_to_all x0 -> x1, waiting for transfers between devices: none -> 4.68 us  [local(): lax.all_to_all(jnp.stack([query for _ in range(lax.axis_size('seq'))]), '...]
  transfers between devices with their start and end apart: 1 -> 2, of which waited for: 1 -> 2; matrix products, arithmetic and copies ran while one was open for 0% -> 5% of each run, Pallas kernels for 0% -> 0%
where the time goes in v1:
time: 170 us
  waiting for transfers between devices  77.9 us (46%)
  blocking collectives  30 us (18%)
  local copies, waits for them, and re-layouts  20.5 us (12%)
  between operations  13.6 us (8%)
  starting transfers between devices  12.1 us (7%)
  matrix products  9.9 us (6%)
  other arithmetic  5.77 us (3%)
    all_gather x1, waiting for transfers between devices, local(): all_parts = lax.all_gather(packed, 'seq', axis=0, tiled=True)  73.2 us
    psum x1, blocking collectives, local(): attn_out = lax.psum(partial_out, 'tensor')  17.4 us
    all_gather x1, blocking collectives, local(): gathered = lax.all_gather(hidden, 'tensor', axis=1, tiled=True)  12.7 us
    all_to_all x1, starting transfers between devices, local(): lax.all_to_all(jnp.stack([query for _ in range(lax.axis_size('seq'))]), '...  12.1 us
    all_to_all x1, waiting for transfers between devices, local(): lax.all_to_all(jnp.stack([query for _ in range(lax.axis_size('seq'))]), '...  4.68 us
    slice x2, local copies, waits for them, and re-layouts, local(): all_parts[:, width_local + heads_local:width_local + 2 * heads_local]  4.38 us
    slice x1, local copies, waits for them, and re-layouts, local(): page_cache[:, :, 1, :].reshape(pages, page_len, heads_local, HEAD_DIM)  4.28 us
  transfers between devices with their start and end apart: 2, of which 2 were waited for; matrix products, arithmetic and copies ran while one was open for 5% of the time, Pallas kernels for 0%

profile of v1, /device:TPU:4, one launch (start us, length us, event | category | flops | bytes accessed | tf_op | source)
XLA Modules:
  0.0 169.9 jit_solution(17696709360320352634)
XLA Ops:
  6.5 0.9 mul.88
  7.4 12.7 %all-gather = bf16[4,320,8]{1,2,0:T(8,128)(2,1)S(1)} all-gather(bf16[1,320,8]{1,2,0:T(8,128)(2,1)} %bitcast.59), channel_id=1, replica_groups=mesh['seq'=64,'tensor'=4] {'tensor'}, dimensions={0}, use_global_device_ids=true | all-gather | bytes 25600 | tf_op jit(solution)/shard_map/all_gather | solution.py:36
  20.3 0.7 fusion.21
  21.1 0.6 copy-done.3
  22.3 1.1 reshape.197
  23.4 12.1 %all-to-all-start = ((bf16[64,2,1280]{2,1,0:T(2,128)(2,1)}), bf16[64,2,1280]{2,1,0:T(2,128)(2,1)S(1)}, u32[]{:S(2)}, u32[]{:S(2)}) async-start(bf16[64,2,1280]{2,1,0:T(2,128)(2,1)} %reshape.197), calls=%async_computation | async-start | bytes 655360 | tf_op jit(solution)/shard_map/all_to_all | solution.py:54
  35.7 4.3 %fusion.18 = (bf16[24,128,1,320]{1,3,2,0:T(8,128)(2,1)}, bf16[24,128,1,320]{1,3,2,0:T(8,128)(2,1)}) fusion(bf16[24,128,2,320]{1,3,2,0:T(8,128)(2,1)} %param.17), kind=kLoop, calls=%fused_computation.59 | loop fusion | bytes 7864320 | tf_op jit(solution)/shard_map/slice | solution.py:61
  40.0 0.7 gather_fusion
  40.7 2.2 %fusion = f32[24,128,5]{1,2,0:T(8,128)S(1)} fusion(bf16[24,128,5,64]{1,3,2,0:T(8,128)(2,1)} %bitcast.54), kind=kLoop, calls=%fused_computation.4 | loop fusion | flops 2933760 | bytes 2027520 | tf_op jit(solution)/shard_map/reduce_sum | solution.py:14
  43.0 0.7 add_sqrt_fusion
  43.7 4.7 %all-to-all-done = bf16[64,2,1280]{2,1,0:T(2,128)(2,1)S(1)} async-done(((bf16[64,2,1280]{2,1,0:T(2,128)(2,1)}), bf16[64,2,1280]{2,1,0:T(2,128)(2,1)S(1)}, u32[]{:S(2)}, u32[]{:S(2)}) %all-to-all-start) | async-done | bytes 327712 | tf_op jit(solution)/shard_map/all_to_all | solution.py:54
  49.4 1.2 gather_fusion.1
  50.5 2.3 %fusion.3 = f32[24,5,1,128]{3,2,1,0:T(1,128)S(1)} fusion(bf16[24,128,5,64]{1,3,2,0:T(8,128)(2,1)} %bitcast.55, f32[5,64]{1,0:T(8,128)S(1)} %mul.88, f32[24,128,5]{1,2,0:T(8,128)} %add_sqrt_fusion, bf16[24,5,64,1]{2,1,0,3:T(8,128)(2,1)} %bitcast.58), kind=kOutput, calls=%fused_computation.7 | convolution fusion | flops 5898240 | bytes 2105600 | tf_op jit(solution)/shard_map/sphd,shd->shp/dot_general | solution.py:62
  53.3 2.6 %fusion.9 = f32[24,5,1,64]{3,2,1,0:T(1,128)S(1)} fusion(bf16[24,128,5,64]{1,3,2,0:T(8,128)(2,1)} %bitcast.56, bf16[24,5,128,1]{2,0,1,3:T(8,128)(2,1)S(1)} %get-tuple-element.15), kind=kOutput, calls=%fused_computation.21 | convolution fusion | flops 1966080 | bytes 2027520 | tf_op jit(solution)/shard_map/shp,sphd->shd/dot_general | solution.py:72
  56.1 0.7 pad_maximum_fusion
  56.9 73.2 %all-gather.3.cloned.1.call-done = f32[1536,331]{1,0:T(8,128)} async-done(((f32[24,331]{1,0:T(8,128)}), f32[1536,331]{1,0:T(8,128)}) %all-gather.3.cloned.1.call-update) | async-done | bytes 2033680 | tf_op jit(solution)/shard_map/all_gather | solution.py:78
  130.1 3.0 %fusion.19 = (f32[1536,5]{1,0:T(8,128)}, f32[1536,5]{1,0:T(8,128)S(1)}) fusion(f32[1536,331]{1,0:T(8,128)} %all-gather.3.cloned.1.call-done), kind=kLoop, calls=%fused_computation.60 | loop fusion | bytes 122880 | tf_op jit(solution)/shard_map/slice | solution.py:81
  133.1 1.4 copy.69
  134.7 1.6 slice_reduce_fusion
  137.3 3.0 %copy.68 = f32[1536,320]{0,1:T(8,128)} copy(f32[1536,320]{1,0:T(8,128)} %bitcast.52) | data formatting | bytes 3932160 | tf_op jit(solution)/shard_map/slice | solution.py:79
  140.3 3.3 %convolution_bitcast_fusion = f32[8,5,64]{2,0,1:T(8,128)S(1)} fusion(f32[1536,5,64]{0,2,1:T(8,128)} %bitcast.53, f32[8,5]{0,1:T(8,128)S(1)} %multiply_maximum_fusion, f32[1536,5]{0,1:T(8,128)S(1)} %copy.69, pred[8,1536]{1,0:T(8,128)(4,1)S(1)} %broadcast_compare_fusion), kind=kOutput, calls=%fused_computation.8 | convolution fusion | flops 47308800 | bytes 2019488 | tf_op jit(solution)/shard_map/rsh,shd->rhd/dot_general | solution.py:91
  143.7 0.9 fusion.14
  144.6 17.4 %psum.7 = f32[8,1280]{1,0:T(8,128)S(1)} all-reduce(f32[8,1280]{1,0:T(8,128)S(1)} %fusion.14), channel_id=1, replica_groups=mesh['seq'=64,'tensor'=4] {'tensor'}, use_global_device_ids=true, to_apply=%region_8.9 | all-reduce | flops 10240 | bytes 81920 | tf_op jit(solution)/shard_map/psum | solution.py:104
  162.3 0.7 fusion.13
  (60 shorter events, 4.2 us)
Async XLA Ops:
  6.5 13.7 %copy-start = (bf16[1280,3,320]{0,2,1:T(8,128)(2,1)S(1)}, bf16[1280,3,320]{0,2,1:T(8,128)(2,1)}, u32[]{:S(2)}) copy-start(bf16[1280,3,320]{0,2,1:T(8,128)(2,1)} %param.10) | copy-start | bytes 7372804
  20.2 15.3 %copy-start.5 = (s32[24]{0:T(128)S(1)}, s32[24]{0:T(128)}, u32[]{:S(2)}) copy-start(s32[24]{0:T(128)} %param.16) | copy-start | bytes 292
  20.3 15.3 %copy-start.6 = (s32[24]{0:T(128)S(1)}, s32[24]{0:T(128)}, u32[]{:S(2)}) copy-start(s32[24]{0:T(128)} %param.15) | copy-start | bytes 292
  21.0 0.6 copy-start.3
  23.4 25.0 %all-to-all-start = ((bf16[64,2,1280]{2,1,0:T(2,128)(2,1)}), bf16[64,2,1280]{2,1,0:T(2,128)(2,1)S(1)}, u32[]{:S(2)}, u32[]{:S(2)}) async-start(bf16[64,2,1280]{2,1,0:T(2,128)(2,1)} %reshape.197), calls=%async_computation | async-start | bytes 655360 | tf_op jit(solution)/shard_map/all_to_all | solution.py:54
  35.5 94.6 %all-gather.3.cloned.1.call-start = ((), (), s32[]{:S(2)}) async-start(), calls=%async_computation.1 | async-start | bytes 2396160 | tf_op jit(solution)/shard_map/all_gather | solution.py:78
  35.7 4.3 %copy-start.1 = (s32[512]{0:T(512)S(1)}, s32[512]{0:T(512)}, u32[]{:S(2)}) copy-start(s32[512]{0:T(512)} %param.14) | copy-start | bytes 6148
  137.3 6.5 %copy-start.2 = (bf16[320,1280]{1,0:T(8,128)(2,1)S(1)}, bf16[320,1280]{1,0:T(8,128)(2,1)}, u32[]{:S(2)}) copy-start(bf16[320,1280]{1,0:T(8,128)(2,1)} %param.11) | copy-start | bytes 2457604
  140.3 21.8 %copy-start.4 = (f32[1280]{0:T(1024)S(1)}, f32[1280]{0:T(1024)}, u32[]{:S(2)}) copy-start(f32[1280]{0:T(1024)} %param.13) | copy-start | bytes 15364
Sparse Core Ops, SparseCore 0:
  56.9 73.1 all-gather.2
